TPU v7x, 32 devices: a whole 2x2x4 slice. The times are simulated.
32 devices in a mesh: gx: 8 (over z, y), gy: 4 (over x, core).
Axes of the slice: x: 2, y: 2, z: 4, core: 2. Of those that a mesh axis runs over, the one named last changes fastest.
Arguments:
- queries: bfloat16 [8, 768, 2560], P('gx', 'gy'), may hold values from -7 to 7
- new_kv: bfloat16 [8, 768, 512], P('gx', 'gy'), may hold values from -7 to 7
- cache_pool: bfloat16 [8, 2048, 512], P('gx', 'gy'), may hold values from -6 to 6
- lengths: int32 [8], P('gx'), may hold values from 0 to 32768, as said below
- owner: int32 [8, 4], P('gx'), may hold values from 0 to 3, each once within a row
- w_out: bfloat16 [2560, 2560], P(None, ('gx', 'gy')), may hold values from -0.125 to 0.125
- last_residual: bfloat16 [8, 2560], P(None, ('gx', 'gy')), may hold values from -6 to 6
- norm_gain: bfloat16 [2560], replicated, may hold values from 0.5 to 1.5
- head: bfloat16 [256000, 2560], P(('gx', 'gy')), may hold values from -11 to 11
- targets: int32 [8], replicated, may hold values from 0 to 255999
Outputs:
- mixed_out: bfloat16 [8, 768, 2560], P('gx', 'gy')
- new_cache: bfloat16 [8, 2048, 512], P('gx', 'gy')
- log_norm: float32 [8], replicated
- top_logit: float32 [8], replicated
- target_logprob: float32 [8], replicated
Inputs may be any that keep to these rules, and one draw needn't show every extreme that they name: `lengths`: in every draw one request has seen 32768 tokens and one has seen none. `owner`: each row names every block index once.
All inputs are finite; a program needn't handle non-finite values.
Results may differ from a plain program's by a relative error of at most 0.0042.
Values may be sent and summed in bfloat16 or wider, within the bound.
No kernel may reach another device: no remote copies, remote signals or barrier semaphores. Data moves between devices by JAX's collectives and lax.ppermute only.
A program may use at most 128 MiB of HBM per device.

v0:
```python
import math
import jax
import jax.numpy as jnp
from jax import lax
from jax.sharding import PartitionSpec as P


def on_device(
    queries, new_kv, cache_pool, lengths, owner, w_out, last_residual, norm_gain, head, targets
):
    req_local, new_local, model_cols = queries.shape
    slot_count = cache_pool.shape[1]
    entry_width = new_kv.shape[2]
    head_dim = entry_width // 2
    head_count = model_cols // head_dim
    group_pos = lax.axis_size("gy")
    my_index = lax.axis_index("gy")
    new_total = new_local * group_pos
    window_len = slot_count * group_pos
    keep_len = window_len - new_total
    score_scale = 1.0 / math.sqrt(head_dim)
    query_heads = queries.reshape(req_local, new_local, head_count, head_dim)
    query_pos = my_index * new_local + jnp.arange(new_local, dtype=jnp.int32)
    first_slot = window_len - lengths
    block_ids = jnp.arange(group_pos, dtype=jnp.int32)
    matches = owner[:, :, None] == block_ids[None, None, :]
    logical = jnp.sum(jnp.where(matches, block_ids[None, :, None], 0), axis=1)
    own_block = lax.dynamic_index_in_dim(logical, my_index, axis=1, keepdims=False)
    slot_ids = jnp.arange(slot_count, dtype=jnp.int32)
    new_ids = jnp.arange(new_local, dtype=jnp.int32)
    target_slot = own_block[:, None] * slot_count + slot_ids[None, :]
    from_old = target_slot < keep_len
    old_slot = jnp.minimum(target_slot + new_total, window_len - 1)
    old_block = jnp.take_along_axis(owner, old_slot // slot_count, axis=1)
    pool_row = old_block * slot_count + old_slot % slot_count
    new_row = jnp.maximum(target_slot - keep_len, 0)
    source_cache = jnp.where(from_old, pool_row, -1)
    source_new = jnp.where(from_old, -1, new_row)

    def cache_keys(shard_ids):
        chosen = jnp.take(logical, shard_ids, axis=1)
        slot_pos = (chosen[:, :, None] * slot_count + slot_ids[None, None, :]).reshape(
            req_local, -1
        )
        return (slot_pos[:, None, :] >= query_pos[None, :, None]) & (
            slot_pos[:, None, :] >= first_slot[:, None, None]
        )

    def new_keys(shard_ids):
        positions = (shard_ids[:, None] * new_local + new_ids[None, :]).reshape(-1)
        seen_new = positions[None, :] <= query_pos[:, None]
        return seen_new[None]

    def attend(carried, key_rows, visible):
        running_max, weight_sum, accumulated = carried
        scores = (
            jnp.einsum(
                "rthd,rnd->rthn",
                query_heads,
                key_rows[:, :, :head_dim],
                preferred_element_type=jnp.float32,
            )
            * score_scale
        )
        allowed = visible[:, :, None, :]
        block_max = jnp.max(jnp.where(allowed, scores, -1e30), axis=3)
        new_max = jnp.maximum(running_max, block_max)
        weights = jnp.where(allowed, jnp.exp(scores - new_max[..., None]), 0.0)
        rescale = jnp.exp(running_max - new_max)
        weight_sum = rescale * weight_sum + jnp.sum(weights, axis=3)
        accumulated = rescale[..., None] * accumulated + jnp.einsum(
            "rthn,rnd->rthd",
            weights.astype(jnp.bfloat16),
            key_rows[:, :, head_dim:],
            preferred_element_type=jnp.float32,
        )
        return (new_max, weight_sum, accumulated)

    def copy_rows(fresh_block, part_rows, source, base_row):
        local_row = source - base_row
        inside = (local_row >= 0) & (local_row < part_rows.shape[1])
        clipped = jnp.clip(local_row, 0, part_rows.shape[1] - 1)
        picked = jnp.take_along_axis(part_rows, clipped[:, :, None], axis=1)
        return jnp.where(inside[:, :, None], picked, fresh_block)

    def make_step(shard_width, source, layout_kind, carried, shard_rows):
        shard_count = shard_rows.shape[1] // shard_width
        group_size = math.gcd(shard_count, 4)

        def turn_body(turn_index, inner_state):
            offset = turn_index * group_size * shard_width
            part_rows = lax.dynamic_slice_in_dim(shard_rows, offset, group_size * shard_width, 1)
            shard_ids = turn_index * group_size + jnp.arange(group_size, dtype=jnp.int32)
            if layout_kind == "cache":
                key_rows = part_rows
                visible = cache_keys(shard_ids)
            else:
                key_rows = part_rows
                visible = new_keys(shard_ids)
            softmax_state = lax.cond(
                jnp.any(visible),
                lambda state: attend(state, key_rows, visible),
                lambda state: state,
                inner_state[:3],
            )
            fresh_block = copy_rows(inner_state[3], part_rows, source, offset)
            return softmax_state + (fresh_block,)

        return lax.fori_loop(0, shard_count // group_size, turn_body, carried)

    initial = (
        jnp.full((req_local, new_local, head_count), -1e30, jnp.float32),
        jnp.zeros((req_local, new_local, head_count), jnp.float32),
        jnp.zeros((req_local, new_local, head_count, head_dim), jnp.float32),
        jnp.zeros((req_local, slot_count, entry_width), jnp.bfloat16),
    )
    carried = make_step(
        slot_count,
        source_cache,
        "cache",
        initial,
        lax.all_gather(cache_pool, "gy", axis=1, tiled=True),
    )
    carried = make_step(
        new_local, source_new, "new", carried, lax.all_gather(new_kv, "gy", axis=1, tiled=True)
    )
    running_max, weight_sum, accumulated, fresh_block = carried
    mixed_out = (
        (accumulated / weight_sum[..., None])
        .astype(jnp.bfloat16)
        .reshape(req_local, new_local, model_cols)
    )
    last_local = mixed_out[:, new_local - 1, :]
    group_req = lax.axis_size("gx")
    holder = (my_index == group_pos - 1).astype(jnp.float32)
    padded = jnp.zeros((req_local * group_req, model_cols), jnp.float32)
    padded = lax.dynamic_update_slice_in_dim(
        padded, last_local.astype(jnp.float32) * holder, lax.axis_index("gx") * req_local, 0
    )
    last_mixed = lax.psum(padded, ("gx", "gy")).astype(jnp.bfloat16)
    last_hidden = (
        last_residual.astype(jnp.float32)
        + jnp.dot(last_mixed, w_out, preferred_element_type=jnp.float32)
    ).astype(jnp.bfloat16)
    full_hidden = lax.all_gather(last_hidden, ("gx", "gy"), axis=1, tiled=True).astype(jnp.float32)
    normed = (
        full_hidden
        * lax.rsqrt(jnp.mean(full_hidden * full_hidden, axis=1, keepdims=True) + 1e-06)
        * norm_gain.astype(jnp.float32)
    ).astype(jnp.bfloat16)
    logits = lax.dot_general(
        normed, head, (((1,), (1,)), ((), ())), preferred_element_type=jnp.float32
    )
    vocab_local = head.shape[0]
    local_target = targets - lax.axis_index(("gx", "gy")) * vocab_local
    target_hit = jnp.arange(vocab_local, dtype=jnp.int32)[None, :] == local_target[:, None]
    picked = jnp.sum(jnp.where(target_hit, logits, 0.0), axis=1)
    local_top = jnp.max(logits, axis=1)
    top_logit = lax.pmax(local_top, ("gx", "gy"))
    exp_total, picked = lax.psum(
        (jnp.sum(jnp.exp(logits - top_logit[:, None]), axis=1), picked), ("gx", "gy")
    )
    log_norm = top_logit + jnp.log(exp_total)
    return (mixed_out, fresh_block, log_norm, top_logit, picked - log_norm)


def solution(mesh):
    placed = (
        P("gx", "gy", None),
        P("gx", "gy", None),
        P("gx", "gy", None),
        P("gx"),
        P("gx", None),
        P(None, ("gx", "gy")),
        P(None, ("gx", "gy")),
        P(),
        P(("gx", "gy"), None),
        P(),
    )
    return jax.shard_map(
        on_device,
        mesh=mesh,
        in_specs=placed,
        out_specs=(P("gx", "gy", None), P("gx", "gy", None), P(), P(), P()),
        check_vma=False,
    )
```

profile of v0, /device:TPU:0, one launch (start us, length us, event | category | flops | bytes accessed | tf_op | source)
XLA Modules:
  0.0 262.6 jit_solution(15581894182387955175)
XLA Ops:
  7.2 0.0 all-gather.3.cloned.1.call-start
  7.2 0.7 all-gather.3.cloned.1.call-update
  8.6 1.5 copy.34
  10.2 0.7 select_reduce_fusion.3
  10.9 0.6 gather_fusion
  11.6 0.1 add.795
  11.6 1.1 compare_and_fusion
  13.4 0.1 iota_add_fusion
  13.5 0.1 add.792
  13.6 0.8 compare_reduce_fusion
  15.0 0.7 convert_element_type.62
  15.7 0.6 dynamic-slice.3
  17.0 1.5 fusion.55
  18.4 2.6 compare_select_fusion
  21.1 14.6 %all_gather.10 = bf16[1,768,512]{2,1,0:T(8,128)(2,1)S(1)} all-gather(bf16[1,192,512]{2,1,0:T(8,128)(2,1)} %param.15), channel_id=1, replica_groups=mesh['gx'=8,'gy'=4] {'gy'}, dimensions={1}, use_global_device_ids=true | all-gather | bytes 983040 | tf_op jit(solution)/shard_map/all_gather | solution.py:125
  35.7 2.6 gather_fusion.1
  38.3 1.4 broadcast_in_dim.173
  39.7 0.6 compare_and_fusion.3
  40.3 2.6 compare_select_fusion.3
  42.9 0.6 pad_clamp_fusion
  43.5 0.6 compare_and_fusion.2
  44.1 0.6 compare_and_fusion.1
  44.7 15.8 %conditional.2 = ((f32[1,192,10]{1,2,0:T(8,128)S(1)}, f32[1,192,10]{1,2,0:T(8,128)S(1)}, f32[1,192,10,256]{3,1,2,0:T(8,128)})) conditional(s32[]{:T(128)} %convert_element_type.54, (f32[1,192,10]{1,2,0:T(8,128)S(1)}, f32[1,192,10]{1,2,0:T(8,128)S(1)}, f32[1,192,10,256]{3,1,2,0:T(8,128)}) %tuple.31, (pred[1,192,2048]{2,1,0:T(8,128)(4,1)S(1)}, ...), branch_computations={%region_3.4_spmd, %region_4.7_spmd} | conditional | flops 4070774272 | bytes 63906876 | solution.py:100
  44.7 5.7 %select_reduce_fusion = (f32[192,10]{0,1:T(8,128)S(1)}, f32[192,10,2048]{2,0,1:T(8,128)S(1)}) fusion(pred[192,2048]{1,0:T(8,128)(4,1)S(1)} %bitcast.103, bf16[1,2048,512]{2,1,0:T(8,128)(2,1)} %get-tuple-element.118, bf16[1,192,10,256]{1,3,2,0:T(8,128)(2,1)S(1)} %get-tuple-element.209), kind=kOutput, calls=%fused_computation.4 | convolution fusion | flops 2025060480 | bytes 18161152 | tf_op jit(solution)/shard_map/while/body/eval_jaxpr/cond/branch_1_fun/rthd,rnd->rthn/dot_general | solution.py:57
  50.4 5.4 %bitcast_add_fusion = f32[1,192,10,256]{3,1,2,0:T(8,128)} fusion(f32[1,192,10,256]{3,1,2,0:T(8,128)} %get-tuple-element.120, f32[192,10,2048]{2,0,1:T(8,128)S(1)} %get-tuple-element.243, f32[192,10]{0,1:T(8,128)S(1)} %bitcast.109, pred[192,2048]{1,0:T(8,128)(4,1)S(1)} %bitcast.104, bf16[1,2048,512]{2,1,0:T(8,128)(2,1)S(1)} %copy-done.2, ...), kind=kOutput, calls=%fused_computation.9 | convolution fusion | flops 2029977600 | bytes 21135360 | tf_op jit(solution)/shard_map/while/body/eval_jaxpr/cond/branch_1_fun/rthn,rnd->rthd/dot_general | solution.py:71
  55.8 4.7 %fusion.1 = f32[192,10]{0,1:T(8,128)S(1)} fusion(f32[192,10,2048]{2,0,1:T(8,128)S(1)} %get-tuple-element.243, f32[192,10]{0,1:T(8,128)S(1)} %bitcast.110, pred[192,2048]{1,0:T(8,128)(4,1)S(1)} %bitcast.105), kind=kLoop, calls=%fused_computation.6 | loop fusion | flops 15726720 | bytes 16137216 | tf_op jit(solution)/shard_map/while/body/eval_jaxpr/cond/branch_1_fun/reduce_sum | solution.py:70
  60.5 7.6 %conditional.3 = ((f32[1,192,10]{1,2,0:T(8,128)S(1)}, f32[1,192,10,256]{3,1,2,0:T(8,128)})) conditional(s32[]{:T(128)} %convert_element_type.53, (f32[1,192,10]{1,2,0:T(8,128)S(1)}, f32[1,192,10,256]{3,1,2,0:T(8,128)}) %tuple.33, (s32[768]{0:T(1024)S(1)}, s32[192]{0:T(256)S(1)}, bf16[1,192,10,256]{1,3,2,0:T(8,128)(2,1)S(1)}, ...), branch_computations={%region_7.8_spmd, %region_8.11_spmd} | conditional | flops 1527307776 | bytes 24442648 | solution.py:100
  60.5 0.1 broadcast_compare_fusion
  60.6 1.7 select_reduce_fusion.1
  62.4 3.7 %bitcast_add_fusion.2 = f32[1,192,10,256]{3,1,2,0:T(8,128)} fusion(f32[1,192,10,256]{3,1,2,0:T(8,128)} %get-tuple-element.138, f32[192,10,768]{2,0,1:T(8,128)S(1)} %get-tuple-element.241, f32[192,10]{0,1:T(8,128)S(1)} %get-tuple-element.239, pred[192,768]{1,0:T(8,128)(4,1)S(1)} %broadcast_compare_fusion, f32[192,10]{0,1:T(8,128)S(1)} %get-tuple-element.238, ...), kind=kOutput, calls=%fused_computation.31 | convolution fusion | flops 761856000 | bytes 10403840 | tf_op jit(solution)/shard_map/while/body/eval_jaxpr/cond/branch_1_fun/rthn,rnd->rthd/dot_general | solution.py:71
  66.1 1.7 fusion.17
  68.1 1.9 divide_convert_fusion
  70.0 0.6 copy.37
  70.6 1.4 copy.39
  71.9 0.6 multiply_reduce_fusion
  72.6 0.3 dynamic_update_slice.3
  72.8 41.4 %psum.21 = bf16[8,2560]{1,0:T(8,128)(2,1)S(1)} all-reduce(f32[8,2560]{1,0:T(8,128)S(1)} %dynamic_update_slice.3), channel_id=1, replica_groups=mesh['gx'=8,'gy'=4] {'gx','gy'}, use_global_device_ids=true, to_apply=%region_11.12 | all-reduce | flops 20480 | bytes 122880 | tf_op jit(solution)/shard_map/psum | solution.py:140
  114.3 0.2 fusion.37
  114.5 40.6 %all-gather = bf16[32,80,8]{1,2,0:T(8,128)(2,1)S(1)} all-gather(bf16[1,80,8]{1,2,0:T(8,128)(2,1)S(1)} %fusion.37), channel_id=1, replica_groups=mesh['gx'=8,'gy'=4] {'gx','gy'}, dimensions={0}, use_global_device_ids=true | all-gather | bytes 42240 | tf_op jit(solution)/shard_map/all_gather | solution.py:145
  155.1 0.1 reshape.940
  155.2 0.1 multiply_reduce_fusion.1
  155.4 17.4 %fusion.56 = (f32[8]{0:T(128)S(1)}, f32[8,8000]{1,0:T(8,128)S(1)}) fusion(bf16[8000,2560]{1,0:T(8,128)(2,1)} %param.22, f32[2560,8]{0,1:T(8,128)S(1)} %reshape.940, f32[2560]{0:T(1024)S(1)} %convert_element_type.62, f32[8]{0:T(128)S(1)} %add_rsqrt_fusion), kind=kOutput, calls=%fused_computation.123 | convolution fusion | flops 327805440 | bytes 41308224 | tf_op jit(solution)/shard_map/dot_general | solution.py:151
  172.7 36.9 %pmax.7 = f32[8]{0:T(128)S(1)} all-reduce(f32[8]{0:T(128)S(1)} %get-tuple-element.250), channel_id=1, replica_groups=mesh['gx'=8,'gy'=4] {'gx','gy'}, use_global_device_ids=true, to_apply=%region_14.15 | all-reduce | flops 8 | bytes 64 | tf_op jit(solution)/shard_map/pmax | solution.py:159
  209.7 0.3 select_reduce_fusion.2
  209.9 41.2 %all-reduce = (f32[8]{0:T(128)S(1)}, f32[8]{0:T(128)S(1)}) all-reduce(f32[8]{0:T(128)S(1)} %get-tuple-element.227, f32[8]{0:T(128)S(1)} %get-tuple-element.226), channel_id=1, replica_groups=mesh['gx'=8,'gy'=4] {'gx','gy'}, use_global_device_ids=true, to_apply=%region_16.17 | all-reduce | flops 16 | bytes 128 | tf_op jit(solution)/shard_map/psum | solution.py:160
  251.2 0.5 fusion.53
  251.7 2.1 gather_fusion.2
  253.8 1.9 fusion.39
  (36 shorter events, 0.2 us)
Async XLA Ops:
  7.2 107.1 %copy-start = (bf16[2560,80]{0,1:T(8,128)(2,1)S(1)}, bf16[2560,80]{0,1:T(8,128)(2,1)}, u32[]{:S(2)}) copy-start(bf16[2560,80]{0,1:T(8,128)(2,1)} %param.19) | copy-start | bytes 1228804
  7.2 36.3 %copy-start.6 = (s32[8]{0:T(128)S(1)}, s32[8]{0:T(128)}, u32[]{:S(2)}) copy-start(s32[8]{0:T(128)} %param.23) | copy-start | bytes 100
  7.2 37.5 %all-gather.3.cloned.1.call-start = ((), (), s32[]{:S(2)}) async-start(), calls=%async_computation | async-start | bytes 2621440 | tf_op jit(solution)/shard_map/all_gather | solution.py:122
  44.7 5.7 %copy-start.2 = (bf16[1,2048,512]{2,1,0:T(8,128)(2,1)S(1)}, bf16[1,2048,512]{2,1,0:T(8,128)(2,1)}, u32[]{:S(2)}) copy-start(bf16[1,2048,512]{2,1,0:T(8,128)(2,1)} %get-tuple-element.118) | copy-start | bytes 6291460 | tf_op jit(solution)/shard_map/while/body/eval_jaxpr/cond
  68.1 46.2 %copy-start.4 = (bf16[8,80]{1,0:T(8,128)(2,1)S(1)}, bf16[8,80]{1,0:T(8,128)(2,1)}, u32[]{:S(2)}) copy-start(bf16[8,80]{1,0:T(8,128)(2,1)} %param.20) | copy-start | bytes 3844
  155.3 96.3 %copy-start.1 = (bf16[1,2048,512]{2,1,0:T(8,128)(2,1)S(1)}, bf16[1,2048,512]{2,1,0:T(8,128)(2,1)}, u32[]{:S(2)}) copy-start(bf16[1,2048,512]{2,1,0:T(8,128)(2,1)} %all-gather.3.cloned.1.call-done) | copy-start | bytes 6291460
  155.3 98.4 %copy-start.3 = (bf16[512,512]{1,0:T(8,128)(2,1)S(1)}, bf16[512,512]{1,0:T(8,128)(2,1)}, u32[]{:S(2)}) copy-start(bf16[512,512]{1,0:T(8,128)(2,1)} %gather_fusion.1) | copy-start | bytes 1572868
  209.7 42.0 %copy-start.5 = (f32[8]{0:T(128)}, f32[8]{0:T(128)S(1)}, u32[]{:S(2)}) copy-start(f32[8]{0:T(128)S(1)} %pmax.7) | copy-start | bytes 100
Sparse Core Ops, SparseCore 0:
  9.6 29.4 all-gather.2
where the time goes:
time: 263 us
  blocking collectives  175 us (67%)
  matrix products  34.1 us (13%)
  other arithmetic  23 us (9%)
  between operations  16.9 us (6%)
  local copies, waits for them, and re-layouts  12.9 us (5%)
    psum x1, blocking collectives, on_device(): last_mixed = lax.psum(padded, ('gx', 'gy')).astype(jnp.bfloat16)  41.4 us
    psum x1, blocking collectives, on_device(): lax.psum((jnp.sum(jnp.exp(logits - top_logit[:, None]), axis=1), picked),...  41.2 us
    all_gather x1, blocking collectives, on_device(): lax.all_gather(last_hidden, ('gx', 'gy'), axis=1, tiled=True)  40.6 us
    pmax x1, blocking collectives, on_device(): top_logit = lax.pmax(local_top, ('gx', 'gy'))  36.9 us
    dot_general x1, matrix products, on_device(): lax.dot_general(normed, head, (((1,), (1,)), ((), ())), preferred_element...  17.4 us
    all_gather x1, blocking collectives, on_device(): lax.all_gather(new_kv, 'gy', axis=1, tiled=True)  14.6 us
    dot_general x2, matrix products, attend(): jnp.einsum('rthn,rnd->rthd', weights.astype(jnp.bfloat16), key_rows[:, :,...  9.09 us
    dot_general x2, matrix products, attend(): jnp.einsum('rthd,rnd->rthn', query_heads, key_rows[:, :, :head_dim], pref...  7.42 us
  transfers between devices with their start and end apart: 1, of which 0 were waited for; matrix products, arithmetic and copies ran while one was open for 7% of the time, Pallas kernels for 0%

commit v1 on v0

--- a/solution.py
+++ b/solution.py
@@ -137,7 +137,7 @@
     padded = lax.dynamic_update_slice_in_dim(
         padded, last_local.astype(jnp.float32) * holder, lax.axis_index("gx") * req_local, 0
     )
-    last_mixed = lax.psum(padded, ("gx", "gy")).astype(jnp.bfloat16)
+    last_mixed = jnp.sum(lax.all_gather(padded, ("gx", "gy")), axis=0).astype(jnp.bfloat16)
     last_hidden = (
         last_residual.astype(jnp.float32)
         + jnp.dot(last_mixed, w_out, preferred_element_type=jnp.float32)

time: 263 us -> 275 us (1.046)
  waiting for transfers between devices: 0.68 us -> 52.5 us
  blocking collectives: 175 us -> 132 us
  local copies, waits for them, and re-layouts: 12.9 us -> 15.9 us
    all_gather x0 -> x1, waiting for transfers between devices: none -> 43.8 us  [on_device(): lax.all_gather(padded, ('gx', 'gy'))]
    psum x1 -> x0, blocking collectives: 41.4 us -> none  [on_device(): last_mixed = lax.psum(padded, ('gx', 'gy')).astype(jnp.bfloat16)]
    all_gather x1, waiting for transfers between devices: 0.01 us -> 7.99 us  [on_device(): lax.all_gather(cache_pool, 'gy', axis=1, tiled=True)]
  transfers between devices with their start and end apart: 1 -> 2, of which waited for: 0 -> 2; matrix products, arithmetic and copies ran while one was open for 7% -> 7% of each run, Pallas kernels for 0% -> 0%
where the time goes in v1:
time: 275 us
  blocking collectives  132 us (48%)
  waiting for transfers between devices  52.5 us (19%)
  matrix products  34.3 us (12%)
  other arithmetic  23.4 us (9%)
  between operations  16.9 us (6%)
  local copies, waits for them, and re-layouts  15.9 us (6%)
    all_gather x1, waiting for transfers between devices, on_device(): lax.all_gather(padded, ('gx', 'gy'))  43.8 us
    psum x1, blocking collectives, on_device(): lax.psum((jnp.sum(jnp.exp(logits - top_logit[:, None]), axis=1), picked),...  41.2 us
    all_gather x1, blocking collectives, on_device(): lax.all_gather(last_hidden, ('gx', 'gy'), axis=1, tiled=True)  39.6 us
    pmax x1, blocking collectives, on_device(): top_logit = lax.pmax(local_top, ('gx', 'gy'))  36.9 us
    dot_general x1, matrix products, on_device(): lax.dot_general(normed, head, (((1,), (1,)), ((), ())), preferred_element...  17.2 us
    all_gather x1, blocking collectives, on_device(): lax.all_gather(new_kv, 'gy', axis=1, tiled=True)  13.9 us
    dot_general x2, matrix products, attend(): jnp.einsum('rthn,rnd->rthd', weights.astype(jnp.bfloat16), key_rows[:, :,...  9.13 us
    all_gather x1, waiting for transfers between devices, on_device(): lax.all_gather(cache_pool, 'gy', axis=1, tiled=True)  7.99 us
  transfers between devices with their start and end apart: 2, of which 2 were waited for; matrix products, arithmetic and copies ran while one was open for 7% of the time, Pallas kernels for 0%

profile of v1, /device:TPU:0, one launch (start us, length us, event | category | flops | bytes accessed | tf_op | source)
XLA Modules:
  0.0 274.8 jit_solution(1033040199129981914)
XLA Ops:
  7.2 0.0 all-gather.4.cloned.1.call-start
  7.2 0.7 all-gather.4.cloned.1.call-update
  7.9 0.0 all-gather.6.cloned.1.call-start
  8.6 1.5 copy.40
  10.2 0.7 select_reduce_fusion.3
  11.0 0.6 gather_fusion
  11.6 0.1 add.793
  11.7 1.1 compare_and_fusion
  13.5 0.1 iota_add_fusion
  13.5 0.1 add.790
  13.6 0.8 compare_reduce_fusion
  15.1 1.5 broadcast_in_dim.173
  16.5 13.9 %all_gather.14 = bf16[1,768,512]{2,1,0:T(8,128)(2,1)S(1)} all-gather(bf16[1,192,512]{2,1,0:T(8,128)(2,1)S(1)} %copy-done.4), channel_id=1, replica_groups=mesh['gx'=8,'gy'=4] {'gy'}, dimensions={1}, use_global_device_ids=true | all-gather | bytes 983040 | tf_op jit(solution)/shard_map/all_gather | solution.py:125
  30.5 8.0 %all-gather.4.cloned.1.call-done = bf16[1,2048,512]{2,1,0:T(8,128)(2,1)} async-done(((bf16[1,512,512]{2,1,0:T(8,128)(2,1)}), bf16[1,2048,512]{2,1,0:T(8,128)(2,1)}) %all-gather.4.cloned.1.call-update) | async-done | bytes 2097168 | tf_op jit(solution)/shard_map/all_gather | solution.py:122
  38.5 15.9 %conditional.2 = ((f32[1,192,10]{1,2,0:T(8,128)S(1)}, f32[1,192,10]{1,2,0:T(8,128)S(1)}, f32[1,192,10,256]{3,1,2,0:T(8,128)})) conditional(s32[]{:T(128)} %convert_element_type.48, (f32[1,192,10]{1,2,0:T(8,128)S(1)}, f32[1,192,10]{1,2,0:T(8,128)S(1)}, f32[1,192,10,256]{3,1,2,0:T(8,128)}) %tuple.31, (pred[1,192,2048]{2,1,0:T(8,128)(4,1)S(1)}, ...), branch_computations={%region_3.4_spmd, %region_4.7_spmd} | conditional | flops 4070774272 | bytes 63906876 | solution.py:100
  38.5 5.8 %select_reduce_fusion = (f32[192,10]{0,1:T(8,128)S(1)}, f32[192,10,2048]{2,0,1:T(8,128)S(1)}) fusion(pred[192,2048]{1,0:T(8,128)(4,1)S(1)} %bitcast.102, bf16[1,2048,512]{2,1,0:T(8,128)(2,1)} %get-tuple-element.118, bf16[1,192,10,256]{1,3,2,0:T(8,128)(2,1)S(1)} %get-tuple-element.209), kind=kOutput, calls=%fused_computation.4 | convolution fusion | flops 2025060480 | bytes 18161152 | tf_op jit(solution)/shard_map/while/body/eval_jaxpr/cond/branch_1_fun/rthd,rnd->rthn/dot_general | solution.py:57
  44.3 5.4 %bitcast_add_fusion = f32[1,192,10,256]{3,1,2,0:T(8,128)} fusion(f32[1,192,10,256]{3,1,2,0:T(8,128)} %get-tuple-element.120, f32[192,10,2048]{2,0,1:T(8,128)S(1)} %get-tuple-element.243, f32[192,10]{0,1:T(8,128)S(1)} %bitcast.108, pred[192,2048]{1,0:T(8,128)(4,1)S(1)} %bitcast.103, bf16[1,2048,512]{2,1,0:T(8,128)(2,1)S(1)} %copy-done.2, ...), kind=kOutput, calls=%fused_computation.9 | convolution fusion | flops 2029977600 | bytes 21135360 | tf_op jit(solution)/shard_map/while/body/eval_jaxpr/cond/branch_1_fun/rthn,rnd->rthd/dot_general | solution.py:71
  49.7 4.7 %fusion.1 = f32[192,10]{0,1:T(8,128)S(1)} fusion(f32[192,10,2048]{2,0,1:T(8,128)S(1)} %get-tuple-element.243, f32[192,10]{0,1:T(8,128)S(1)} %bitcast.109, pred[192,2048]{1,0:T(8,128)(4,1)S(1)} %bitcast.104), kind=kLoop, calls=%fused_computation.6 | loop fusion | flops 15726720 | bytes 16137216 | tf_op jit(solution)/shard_map/while/body/eval_jaxpr/cond/branch_1_fun/reduce_sum | solution.py:70
  54.4 7.5 %conditional.3 = ((f32[1,192,10]{1,2,0:T(8,128)S(1)}, f32[1,192,10,256]{3,1,2,0:T(8,128)})) conditional(s32[]{:T(128)} %convert_element_type.47, (f32[1,192,10]{1,2,0:T(8,128)S(1)}, f32[1,192,10,256]{3,1,2,0:T(8,128)}) %tuple.33, (s32[768]{0:T(1024)S(1)}, s32[192]{0:T(256)S(1)}, bf16[1,192,10,256]{1,3,2,0:T(8,128)(2,1)S(1)}, ...), branch_computations={%region_7.8_spmd, %region_8.11_spmd} | conditional | flops 1527307776 | bytes 24442648 | solution.py:100
  54.4 0.1 broadcast_compare_fusion
  54.6 1.8 select_reduce_fusion.1
  56.4 3.8 %bitcast_add_fusion.2 = f32[1,192,10,256]{3,1,2,0:T(8,128)} fusion(f32[1,192,10,256]{3,1,2,0:T(8,128)} %get-tuple-element.138, f32[192,10,768]{2,0,1:T(8,128)S(1)} %get-tuple-element.241, f32[192,10]{0,1:T(8,128)S(1)} %get-tuple-element.239, pred[192,768]{1,0:T(8,128)(4,1)S(1)} %broadcast_compare_fusion, f32[192,10]{0,1:T(8,128)S(1)} %get-tuple-element.238, ...), kind=kOutput, calls=%fused_computation.31 | convolution fusion | flops 761856000 | bytes 10403840 | tf_op jit(solution)/shard_map/while/body/eval_jaxpr/cond/branch_1_fun/rthn,rnd->rthd/dot_general | solution.py:71
  60.2 1.7 fusion.17
  62.0 3.0 %divide_convert_fusion = bf16[1,192,10,256]{3,1,2,0:T(8,128)(2,1)} fusion(f32[1,192,10,256]{3,1,2,0:T(8,128)} %get-tuple-element.152, f32[192,10]{0,1:T(8,128)S(1)} %bitcast.107), kind=kLoop, calls=%fused_computation.46 | loop fusion | flops 983040 | bytes 2956800 | tf_op jit(solution)/shard_map/convert_element_type | solution.py:130
  64.9 2.4 copy.43
  67.3 2.3 copy.47
  69.7 0.8 fusion.44
  70.5 0.4 dynamic_update_slice.4
  70.9 0.6 copy-done.3
  71.6 0.6 dynamic-slice.3
  72.8 0.6 fusion.56
  73.4 2.6 compare_select_fusion
  76.1 2.6 gather_fusion.1
  78.7 2.6 compare_select_fusion.3
  81.4 2.0 gather_fusion.2
  83.3 2.2 fusion.40
  85.6 43.8 %all-gather.6.cloned.1.call-done = f32[32,8,2560]{2,1,0:T(8,128)} async-done(((f32[1,8,2560]{2,1,0:T(8,128)}), f32[32,8,2560]{2,1,0:T(8,128)}) %all-gather.6.cloned.1.call-update) | async-done | bytes 2621456 | tf_op jit(solution)/shard_map/all_gather | solution.py:140
  129.4 1.9 reduce_sum.71
  131.2 0.3 copy.48
  131.6 0.3 fusion.37
  131.9 39.6 %all-gather = bf16[32,80,8]{1,2,0:T(8,128)(2,1)S(1)} all-gather(bf16[1,80,8]{1,2,0:T(8,128)(2,1)S(1)} %fusion.37), channel_id=1, replica_groups=mesh['gx'=8,'gy'=4] {'gx','gy'}, dimensions={0}, use_global_device_ids=true | all-gather | bytes 42240 | tf_op jit(solution)/shard_map/all_gather | solution.py:145
  171.5 0.1 reshape.927
  171.6 0.1 multiply_reduce_fusion
  171.8 17.2 %fusion.57 = (f32[8]{0:T(128)S(1)}, f32[8,8000]{1,0:T(8,128)S(1)}) fusion(bf16[8000,2560]{1,0:T(8,128)(2,1)} %param.22, f32[2560,8]{0,1:T(8,128)S(1)} %reshape.927, f32[2560]{0:T(1024)S(1)} %convert_element_type.56, f32[8]{0:T(128)S(1)} %add_rsqrt_fusion), kind=kOutput, calls=%fused_computation.124 | convolution fusion | flops 327805440 | bytes 41308224 | tf_op jit(solution)/shard_map/dot_general | solution.py:151
  189.0 36.9 %pmax.7 = f32[8]{0:T(128)S(1)} all-reduce(f32[8]{0:T(128)S(1)} %get-tuple-element.250), channel_id=1, replica_groups=mesh['gx'=8,'gy'=4] {'gx','gy'}, use_global_device_ids=true, to_apply=%region_14.15 | all-reduce | flops 8 | bytes 64 | tf_op jit(solution)/shard_map/pmax | solution.py:159
  225.9 0.3 select_reduce_fusion.2
  226.2 41.2 %all-reduce = (f32[8]{0:T(128)S(1)}, f32[8]{0:T(128)S(1)}) all-reduce(f32[8]{0:T(128)S(1)} %get-tuple-element.227, f32[8]{0:T(128)S(1)} %get-tuple-element.226), channel_id=1, replica_groups=mesh['gx'=8,'gy'=4] {'gx','gy'}, use_global_device_ids=true, to_apply=%region_16.17 | all-reduce | flops 16 | bytes 128 | tf_op jit(solution)/shard_map/psum | solution.py:160
  267.4 0.5 fusion.54
  (45 shorter events, 0.3 us)
Async XLA Ops:
  7.2 124.4 %copy-start = (bf16[2560,80]{0,1:T(8,128)(2,1)S(1)}, bf16[2560,80]{0,1:T(8,128)(2,1)}, u32[]{:S(2)}) copy-start(bf16[2560,80]{0,1:T(8,128)(2,1)} %param.19) | copy-start | bytes 1228804
  7.2 9.4 %copy-start.4 = (bf16[1,192,512]{2,1,0:T(8,128)(2,1)S(1)}, bf16[1,192,512]{2,1,0:T(8,128)(2,1)}, u32[]{:S(2)}) copy-start(bf16[1,192,512]{2,1,0:T(8,128)(2,1)} %param.15) | copy-start | bytes 589828
  7.2 31.3 %all-gather.4.cloned.1.call-start = ((), (), s32[]{:S(2)}) async-start(), calls=%async_computation | async-start | bytes 2621440 | tf_op jit(solution)/shard_map/all_gather | solution.py:122
  7.9 121.4 %all-gather.6.cloned.1.call-start = ((), (), s32[]{:S(2)}) async-start(), calls=%async_computation.1 | async-start | bytes 2703360 | tf_op jit(solution)/shard_map/all_gather | solution.py:140
  38.5 5.9 %copy-start.2 = (bf16[1,2048,512]{2,1,0:T(8,128)(2,1)S(1)}, bf16[1,2048,512]{2,1,0:T(8,128)(2,1)}, u32[]{:S(2)}) copy-start(bf16[1,2048,512]{2,1,0:T(8,128)(2,1)} %get-tuple-element.118) | copy-start | bytes 6291460 | tf_op jit(solution)/shard_map/while/body/eval_jaxpr/cond
  61.9 9.6 %copy-start.6 = (bf16[2560]{0:T(1024)(128)(2,1)S(1)}, bf16[2560]{0:T(1024)(128)(2,1)}, u32[]{:S(2)}) copy-start(bf16[2560]{0:T(1024)(128)(2,1)} %param.21) | copy-start | bytes 15364
  61.9 10.9 %copy-start.5 = (s32[1,4]{1,0:T(1,128)S(1)}, s32[1,4]{1,0:T(1,128)}, u32[]{:S(2)}) copy-start(s32[1,4]{1,0:T(1,128)} %param.18) | copy-start | bytes 52
  62.0 19.3 %copy-start.9 = (s32[8]{0:T(128)S(1)}, s32[8]{0:T(128)}, u32[]{:S(2)}) copy-start(s32[8]{0:T(128)} %param.23) | copy-start | bytes 100
  62.0 19.4 %copy-start.1 = (bf16[1,2048,512]{2,1,0:T(8,128)(2,1)S(1)}, bf16[1,2048,512]{2,1,0:T(8,128)(2,1)}, u32[]{:S(2)}) copy-start(bf16[1,2048,512]{2,1,0:T(8,128)(2,1)} %all-gather.4.cloned.1.call-done) | copy-start | bytes 6291460
  70.9 0.6 copy-start.3
  78.7 52.9 %copy-start.7 = (bf16[8,80]{1,0:T(8,128)(2,1)S(1)}, bf16[8,80]{1,0:T(8,128)(2,1)}, u32[]{:S(2)}) copy-start(bf16[8,80]{1,0:T(8,128)(2,1)} %param.20) | copy-start | bytes 3844
  225.9 42.0 %copy-start.8 = (f32[8]{0:T(128)}, f32[8]{0:T(128)S(1)}, u32[]{:S(2)}) copy-start(f32[8]{0:T(128)S(1)} %pmax.7) | copy-start | bytes 100
Sparse Core Ops, SparseCore 0:
  9.6 28.8 all-gather.3
  71.7 57.6 all-gather.5
